TPU v7x, 128 devices: a whole 4x4x4 slice. The times are simulated.
128 devices in a mesh: req: 8 (over x, core), seq: 16 (over z, y).
Axes of the slice: x: 4, y: 4, z: 4, core: 2. Of those that a mesh axis runs over, the one named last changes fastest.
Arguments:
- hidden: bfloat16 [8, 2048, 2048], P('req', 'seq'), may hold values from -6 to 6
- lengths: int32 [8], replicated, may hold values from 1 to 2048, 10240 in all
- slot_request: int32 [8], replicated, may hold values from 0 to 7, each once
- norm_gain: bfloat16 [2048], replicated, may hold values from 0.099609375 to 1.8984375
- in_weight: bfloat16 [2, 2048, 4096], P(None, 'req', 'seq'), may hold values from -0.125 to 0.125
- conv_weight: bfloat16 [4, 4096], P(None, 'seq'), may hold values from -3 to 3
- conv_bias: bfloat16 [4096], P('seq'), may hold values from -0.5 to 0.5
- xproj_weight: bfloat16 [4096, 160], P('seq'), may hold values from -0.09375 to 0.09375
- dt_weight: bfloat16 [128, 4096], P(None, 'seq'), may hold values from -0.5 to 0.5
- dt_bias: bfloat16 [4096], P('seq'), may hold values from -6.91 to -2.25
- a_log: float32 [16, 4096], replicated, may hold values from -2.3 to 1.39
- skip_gain: float32 [4096], replicated, may hold values from 0.5 to 1.5
- out_weight: bfloat16 [4096, 2048], P('seq', 'req'), may hold values from -0.09375 to 0.09375
Outputs:
- mixed: bfloat16 [8, 2048, 2048], P('req', 'seq')
- final_state: float32 [8, 16, 4096], P('req', None, 'seq')
Inputs may be any that keep to these rules, and one draw needn't show every extreme that they name: `lengths`: each slot's length is at least 1, the longest is exactly 2048, and they sum to 10240. `slot_request`: A permutation of the requests.
All inputs are finite; a program needn't handle non-finite values.
Results may differ from a plain program's by a relative error of at most 0.015.
Values may be sent and summed in bfloat16 or wider, within the bound.
No kernel may reach another device: no remote copies, remote signals or barrier semaphores. Data moves between devices by JAX's collectives and lax.ppermute only.
A program may use at most 128 MiB of HBM per device.

v0:
```python
import jax
import jax.numpy as jnp
from jax import lax
from jax.sharding import PartitionSpec as P

STATE = 16
RANK = 128


def gather_a2a(block, axis, dim):
    count = lax.axis_size(axis)
    copies = jnp.broadcast_to(block[None], (count,) + block.shape)
    stacked = lax.all_to_all(copies, axis, split_axis=0, concat_axis=0, tiled=True)
    moved = jnp.moveaxis(stacked, 0, dim)
    shape = list(block.shape)
    shape[dim] = shape[dim] * count
    return moved.reshape(shape)


def to_blocks(array):
    pieces, length, columns = array.shape
    return jnp.moveaxis(array.reshape(pieces, 16, length // 16, columns), 1, 0)


def from_blocks(array):
    count, pieces, group, columns = array.shape
    return jnp.moveaxis(array, 0, 1).reshape(pieces, count * group, columns)


def piece_scan(rates, values, entry, readout, decay):
    pieces, length, columns = rates.shape
    group = length // 16
    positions = jnp.arange(length, dtype=jnp.int32)
    lower = (positions[None, :] <= positions[:, None]).astype(jnp.float32)
    running = jnp.einsum("rs,psw->prw", lower, rates, precision=lax.Precision.HIGHEST)

    def advance(state, items):
        rate, value, into, outof = items
        outputs = []
        for place in range(group):
            factor = jnp.exp(rate[:, place][:, None, :] * decay[None])
            state = (
                factor * state
                + (rate[:, place] * value[:, place])[:, None, :] * into[:, place][:, :, None]
            )
            outputs.append(jnp.sum(outof[:, place][:, :, None] * state, axis=1))
        return (state, jnp.stack(outputs, axis=1))

    start = jnp.zeros((pieces, decay.shape[0], columns), jnp.float32)
    end_local, local_out = lax.scan(
        advance, start, (to_blocks(rates), to_blocks(values), to_blocks(entry), to_blocks(readout))
    )
    total_decay = jnp.exp(running[:, length - 1][:, None, :] * decay[None])
    return (end_local, from_blocks(local_out), total_decay, running)


def carried_part(running, readout, decay, carry_in):

    def correct(items):
        total, outof = items
        kept = jnp.exp(total[:, :, None, :] * decay[None, None]) * carry_in[:, None]
        return jnp.sum(outof[:, :, :, None] * kept, axis=2)

    return from_blocks(lax.map(correct, (to_blocks(running), to_blocks(readout))))


def per_device(
    hidden,
    lengths,
    slot_request,
    norm_gain,
    in_weight,
    conv_weight,
    conv_bias,
    xproj_weight,
    dt_weight,
    dt_bias,
    a_log,
    skip_gain,
    out_weight,
):
    seq_count = lax.axis_size("seq")
    seq_index = lax.axis_index("seq")
    req_index = lax.axis_index("req")
    rows = hidden.shape[1]
    span = rows * seq_count
    width = in_weight.shape[2]
    taps_count = conv_weight.shape[0]
    state_count = a_log.shape[0]
    tokens = hidden[0].astype(jnp.float32)
    scale = lax.rsqrt(jnp.mean(tokens * tokens, axis=-1, keepdims=True) + 1e-05)
    normed = (tokens * scale * norm_gain.astype(jnp.float32)).astype(jnp.bfloat16)
    w_in = gather_a2a(in_weight, "req", 1)
    w_flat = jnp.concatenate((w_in[0], w_in[1]), axis=1)
    both = jnp.dot(
        lax.all_gather(normed, "seq", axis=0, tiled=True),
        w_flat,
        preferred_element_type=jnp.float32,
    )
    xin = both[:, :width]
    zgate = both[:, width:].astype(jnp.bfloat16)
    padded = jnp.pad(xin, ((taps_count - 1, 0), (0, 0)))
    taps = conv_weight.astype(jnp.float32)
    convolved = conv_bias.astype(jnp.float32) + jnp.zeros_like(xin)
    for tap in range(taps_count):
        convolved = convolved + taps[tap] * padded[tap : tap + span, :]
    inner = jax.nn.silu(convolved).astype(jnp.bfloat16)
    inner_tok = lax.all_to_all(inner, "seq", split_axis=0, concat_axis=1, tiled=True)
    xproj_full = gather_a2a(xproj_weight, "seq", 0)
    dt_full = gather_a2a(dt_weight, "seq", 1)
    dt_bias_full = gather_a2a(dt_bias, "seq", 0)
    proj = jnp.dot(inner_tok, xproj_full, preferred_element_type=jnp.float32)
    length_here = lax.dynamic_index_in_dim(lengths, req_index, 0, keepdims=False)
    positions = seq_index * rows + jnp.arange(rows, dtype=jnp.int32)
    live = (positions < length_here).astype(jnp.float32)
    rate_low = proj[:, :RANK].astype(jnp.bfloat16)
    delta_tok = (
        jax.nn.softplus(
            jnp.dot(rate_low, dt_full, preferred_element_type=jnp.float32)
            + dt_bias_full.astype(jnp.float32)
        )
        * live[:, None]
    )
    w_out = gather_a2a(out_weight, "req", 1)
    decay = -jnp.exp(a_log)
    inner_f = inner_tok.astype(jnp.float32)
    entry = proj[None, :, RANK : RANK + STATE]
    readout = proj[None, :, RANK + STATE :]
    end_local, local_out, total_decay, running = piece_scan(
        delta_tok[None], inner_f[None], entry, readout, decay
    )
    pair = jnp.stack((total_decay[0], end_local[0])).reshape(2, state_count, seq_count, width)
    pair_ch = lax.all_to_all(pair, "seq", split_axis=2, concat_axis=2, tiled=True)
    carry = jnp.zeros((state_count, width), jnp.float32)
    carries = []
    for block in range(seq_count):
        carries.append(carry)
        carry = pair_ch[0, :, block] * carry + pair_ch[1, :, block]
    carry_ch = jnp.stack(carries, axis=1)
    carry_in = lax.all_to_all(carry_ch, "seq", split_axis=1, concat_axis=1, tiled=True).reshape(
        state_count, seq_count * width
    )
    carried = carried_part(running, readout, decay, carry_in[None])
    scanned = ((local_out + carried)[0] + skip_gain * inner_f).astype(jnp.bfloat16)
    scanned_ch = lax.all_to_all(scanned, "seq", split_axis=1, concat_axis=0, tiled=True)
    gated_ch = (scanned_ch.astype(jnp.float32) * jax.nn.silu(zgate.astype(jnp.float32))).astype(
        jnp.bfloat16
    )
    branch = lax.psum_scatter(
        jnp.dot(gated_ch, w_out, preferred_element_type=jnp.float32).astype(jnp.bfloat16),
        "seq",
        scatter_dimension=0,
        tiled=True,
    ).astype(jnp.float32)
    slot_all = gather_a2a(carry[None], "req", 0)
    picked = (slot_request == req_index).astype(jnp.float32)
    final_state = jnp.sum(picked[:, None, None] * slot_all, axis=0, keepdims=True)
    mixed = (tokens + branch).astype(jnp.bfloat16)[None]
    return (mixed, final_state)


def solution(mesh):
    in_specs = (
        P("req", "seq", None),
        P(),
        P(),
        P(),
        P(None, "req", "seq"),
        P(None, "seq"),
        P("seq"),
        P("seq", None),
        P(None, "seq"),
        P("seq"),
        P(),
        P(),
        P("seq", "req"),
    )
    out_specs = (P("req", "seq", None), P("req", None, "seq"))
    return jax.shard_map(
        per_device, mesh=mesh, in_specs=in_specs, out_specs=out_specs, check_vma=False
    )
```

profile of v0, /device:TPU:0, one launch (start us, length us, event | category | flops | bytes accessed | tf_op | source)
XLA Modules:
  0.0 439.4 jit_solution(5524272800325330019)
XLA Ops:
  12.9 4.5 %all-to-all-start = ((bf16[8,2,256,256]{3,2,1,0:T(8,128)(2,1)}), bf16[8,2,256,256]{3,2,1,0:T(8,128)(2,1)S(1)}, u32[]{:S(2)}, u32[]{:S(2)}) async-start(bf16[8,2,256,256]{3,2,1,0:T(8,128)(2,1)} %broadcast_in_dim.25), calls=%async_computation | async-start | bytes 4194304 | tf_op jit(solution)/shard_map/all_to_all | solution.py:13
  19.3 25.3 %all-to-all-done = bf16[8,2,256,256]{3,2,1,0:T(8,128)(2,1)S(1)} async-done(((bf16[8,2,256,256]{3,2,1,0:T(8,128)(2,1)}), bf16[8,2,256,256]{3,2,1,0:T(8,128)(2,1)S(1)}, u32[]{:S(2)}, u32[]{:S(2)}) %all-to-all-start) | async-done | bytes 2097184 | tf_op jit(solution)/shard_map/all_to_all | solution.py:13
  44.6 8.0 %all-to-all-start.4 = ((bf16[16,2,128]{2,1,0:T(2,128)(2,1)}), bf16[16,2,128]{2,1,0:T(2,128)(2,1)S(1)}, u32[]{:S(2)}, u32[]{:S(2)}) async-start(bf16[16,2,128]{2,1,0:T(2,128)(2,1)} %reshape.2341), calls=%async_computation.4 | async-start | bytes 16384 | tf_op jit(solution)/shard_map/all_to_all | solution.py:13
  54.1 6.2 %all-to-all-done.4 = bf16[16,2,128]{2,1,0:T(2,128)(2,1)S(1)} async-done(((bf16[16,2,128]{2,1,0:T(2,128)(2,1)}), bf16[16,2,128]{2,1,0:T(2,128)(2,1)S(1)}, u32[]{:S(2)}, u32[]{:S(2)}) %all-to-all-start.4) | async-done | bytes 8224 | tf_op jit(solution)/shard_map/all_to_all | solution.py:13
  61.5 3.7 all-to-all-start.2
  65.2 33.5 %all-gather.2.cloned.1.call-done = bf16[2048,2048]{1,0:T(8,128)(2,1)} async-done(((bf16[128,2048]{1,0:T(8,128)(2,1)}), bf16[2048,2048]{1,0:T(8,128)(2,1)}) %all-gather.2.cloned.1.call-update) | async-done | bytes 8388624 | tf_op jit(solution)/shard_map/all_gather | solution.py:96
  98.7 7.2 %fusion.29 = f32[2048,512]{1,0:T(8,128)S(1)} fusion(bf16[2048,2048]{1,0:T(8,128)(2,1)} %all-gather.2.cloned.1.call-done, bf16[2048,256]{1,0:T(8,128)(2,1)} %bitcast.737, bf16[2048,256]{1,0:T(8,128)(2,1)S(1)} %bitcast.736), kind=kOutput, calls=%fused_computation.84 | convolution fusion | flops 4299161600 | bytes 14680064 | tf_op jit(solution)/shard_map/dot_general | solution.py:95
  110.2 5.5 %all-to-all-start.1 = ((bf16[16,128,256]{2,1,0:T(8,128)(2,1)}), bf16[16,128,256]{2,1,0:T(8,128)(2,1)S(1)}, u32[]{:S(2)}, u32[]{:S(2)}) async-start(bf16[16,128,256]{2,1,0:T(8,128)(2,1)} %bitcast.691), calls=%async_computation.1 | async-start | bytes 2097152 | tf_op jit(solution)/shard_map/all_to_all | solution.py:108
  115.9 17.4 %all-to-all-done.1 = bf16[16,128,256]{2,1,0:T(8,128)(2,1)S(1)} async-done(((bf16[16,128,256]{2,1,0:T(8,128)(2,1)}), bf16[16,128,256]{2,1,0:T(8,128)(2,1)S(1)}, u32[]{:S(2)}, u32[]{:S(2)}) %all-to-all-start.1) | async-done | bytes 1048608 | tf_op jit(solution)/shard_map/all_to_all | solution.py:108
  134.4 4.5 %all-to-all-start.3 = ((bf16[16,128,256]{1,2,0:T(8,128)(2,1)}), bf16[16,128,256]{1,2,0:T(8,128)(2,1)}, u32[]{:S(2)}, u32[]{:S(2)}) async-start(bf16[16,128,256]{1,2,0:T(8,128)(2,1)} %broadcast_in_dim.27), calls=%async_computation.3 | async-start | bytes 2097152 | tf_op jit(solution)/shard_map/all_to_all | solution.py:13
  140.8 13.7 %all-to-all-done.3 = bf16[16,128,256]{1,2,0:T(8,128)(2,1)} async-done(((bf16[16,128,256]{1,2,0:T(8,128)(2,1)}), bf16[16,128,256]{1,2,0:T(8,128)(2,1)}, u32[]{:S(2)}, u32[]{:S(2)}) %all-to-all-start.3) | async-done | bytes 1048608 | tf_op jit(solution)/shard_map/all_to_all | solution.py:13
  167.5 55.2 %while.24 = (s32[]{:T(128)}, f32[1,16,4096]{2,1,0:T(8,128)S(1)}, f32[16,1,8,4096]{3,2,1,0:T(8,128)}, f32[16,1,8,4096]{3,2,1,0:T(8,128)}, f32[16,4096]{1,0:T(8,12...) while((s32[]{:T(128)}, f32[1,16,4096]{2,1,0:T(8,128)S(1)}, ...), condition=%wide.region_10.11_spmd.clone, body=%wide.region_1.10_spmd.clone.sunk | while | flops 4849667 | bytes 4347896 | solution.py:50
  224.0 3.6 all-to-all-start.5
  228.2 9.5 %all-to-all-done.5 = f32[2,16,16,256]{3,1,0,2:T(8,128)S(1)} async-done(((f32[2,16,16,256]{3,1,0,2:T(8,128)}), f32[2,16,16,256]{3,1,0,2:T(8,128)S(1)}, u32[]{:S(2)}, u32[]{:S(2)}) %all-to-all-start.5) | async-done | bytes 524320 | tf_op jit(solution)/shard_map/all_to_all | solution.py:133
  246.8 3.5 all-to-all-start.6
  250.4 8.6 %all-to-all-done.6 = f32[16,16,256]{2,0,1:T(8,128)S(1)} async-done(((f32[16,16,256]{2,0,1:T(8,128)}), f32[16,16,256]{2,0,1:T(8,128)S(1)}, u32[]{:S(2)}, u32[]{:S(2)}) %all-to-all-start.6) | async-done | bytes 262176 | tf_op jit(solution)/shard_map/all_to_all | solution.py:140
  260.8 38.5 %while.23 = (s32[]{:T(128)}, f32[16,1,8,4096]{3,2,1,0:T(8,128)}, f32[16,1,8,16]{3,2,1,0:T(8,128)S(1)}, f32[16,1,8,4096]{3,2,1,0:T(8,128)}, f32[16,4096]{1,0:T(8,128)S(1)}, /*index=5*/f32[16,16,256]{2,1,0:T(8,128)S(1)}, s32[]{:T(128)}) while((s32[]{:T(128)}, f32[16,1,8,4096]{3,2,1,0:T(8,128)}, f32[16,1,8,16]{3,2,1,0:T(8,128)S(1)}, ...), condition=%wide.region_13.14_spmd, body=%wide.region_11.13_spmd.sunk | while | flops 2064386 | bytes 1837141 | solution.py:64
  304.7 4.0 all-to-all-start.7
  308.8 12.8 %all-to-all-done.7 = bf16[128,16,256]{2,0,1:T(8,128)(2,1)S(1)} async-done(((bf16[128,16,256]{2,0,1:T(8,128)(2,1)}), bf16[128,16,256]{2,0,1:T(8,128)(2,1)S(1)}, u32[]{:S(2)}, u32[]{:S(2)}) %all-to-all-start.7) | async-done | bytes 1048608 | tf_op jit(solution)/shard_map/all_to_all | solution.py:145
  322.7 4.3 all-to-all-start.8
  329.3 13.6 %all-to-all-done.8 = bf16[8,256,256]{1,2,0:T(8,128)(2,1)S(1)} async-done(((bf16[8,256,256]{1,2,0:T(8,128)(2,1)}), bf16[8,256,256]{1,2,0:T(8,128)(2,1)S(1)}, u32[]{:S(2)}, u32[]{:S(2)}) %all-to-all-start.8) | async-done | bytes 1048608 | tf_op jit(solution)/shard_map/all_to_all | solution.py:13
  342.9 5.6 %convolution_convert_fusion = bf16[2048,2048]{1,0:T(8,128)(2,1)} fusion(bf16[2048,256]{1,0:T(8,128)(2,1)S(1)} %fusion.36, bf16[256,2048]{0,1:T(8,128)(2,1)S(1)} %bitcast.692), kind=kOutput, calls=%fused_computation.73 | convolution fusion | flops 2151677952 | bytes 10485760 | tf_op jit(solution)/shard_map/dot_general | solution.py:150
  352.7 6.0 %all-to-all-done.9 = f32[8,1,16,256]{3,2,1,0:T(8,128)S(1)} async-done(((f32[8,1,16,256]{3,2,1,0:T(8,128)}), f32[8,1,16,256]{3,2,1,0:T(8,128)S(1)}, u32[]{:S(2)}, u32[]{:S(2)}) %all-to-all-start.9) | async-done | bytes 131104 | tf_op jit(solution)/shard_map/all_to_all | solution.py:13
  359.3 71.3 %reduce-scatter.2.cloned.1.call-done = bf16[128,2048]{1,0:T(8,128)(2,1)} async-done(((bf16[2048,2048]{1,0:T(8,128)(2,1)}), bf16[128,2048]{1,0:T(8,128)(2,1)}) %reduce-scatter.2.cloned.1.call-update) | async-done | bytes 524304 | tf_op jit(solution)/shard_map/reduce_scatter | solution.py:149
  (362 shorter events, 151.1 us)
Async XLA Ops:
  7.2 4.1 copy-start.5
  7.2 91.6 %all-gather.2.cloned.1.call-start = ((), (), s32[]{:S(2)}) async-start(), calls=%async_computation.11 | async-start | bytes 8912896 | tf_op jit(solution)/shard_map/all_gather | solution.py:96
  12.9 4.6 %copy-start.13 = (bf16[256]{0:T(256)(128)(2,1)S(1)}, bf16[256]{0:T(256)(128)(2,1)}, u32[]{:S(2)}) copy-start(bf16[256]{0:T(256)(128)(2,1)} %param.23) | copy-start | bytes 1540
  12.9 4.6 %copy-start.12 = (bf16[256]{0:T(256)(128)(2,1)S(1)}, bf16[256]{0:T(256)(128)(2,1)}, u32[]{:S(2)}) copy-start(bf16[256]{0:T(256)(128)(2,1)} %param.26) | copy-start | bytes 1540
  12.9 6.4 %copy-start.11 = (bf16[4,256]{1,0:T(4,128)(2,1)S(1)}, bf16[4,256]{1,0:T(4,128)(2,1)}, u32[]{:S(2)}) copy-start(bf16[4,256]{1,0:T(4,128)(2,1)} %param.22) | copy-start | bytes 6148
  12.9 31.7 %all-to-all-start = ((bf16[8,2,256,256]{3,2,1,0:T(8,128)(2,1)}), bf16[8,2,256,256]{3,2,1,0:T(8,128)(2,1)S(1)}, u32[]{:S(2)}, u32[]{:S(2)}) async-start(bf16[8,2,256,256]{3,2,1,0:T(8,128)(2,1)} %broadcast_in_dim.25), calls=%async_computation | async-start | bytes 4194304 | tf_op jit(solution)/shard_map/all_to_all | solution.py:13
  44.6 15.7 %all-to-all-start.4 = ((bf16[16,2,128]{2,1,0:T(2,128)(2,1)}), bf16[16,2,128]{2,1,0:T(2,128)(2,1)S(1)}, u32[]{:S(2)}, u32[]{:S(2)}) async-start(bf16[16,2,128]{2,1,0:T(2,128)(2,1)} %reshape.2341), calls=%async_computation.4 | async-start | bytes 16384 | tf_op jit(solution)/shard_map/all_to_all | solution.py:13
  52.6 7.6 %copy-start.8 = (bf16[256,160]{0,1:T(8,128)(2,1)S(1)}, bf16[256,160]{0,1:T(8,128)(2,1)}, u32[]{:S(2)}) copy-start(bf16[256,160]{0,1:T(8,128)(2,1)} %param.24) | copy-start | bytes 245764
  54.1 44.7 %copy-start.4 = (bf16[1,8,256,256]{3,2,0,1:T(8,128)(2,1)S(1)}, bf16[1,8,256,256]{3,2,0,1:T(8,128)(2,1)}, u32[]{:S(2)}) copy-start(bf16[1,8,256,256]{3,2,0,1:T(8,128)(2,1)} %get-tuple-element.265) | copy-start | bytes 3145732
  61.5 48.7 %all-to-all-start.2 = ((bf16[16,256,160]{1,2,0:T(8,128)(2,1)}), bf16[16,256,160]{1,2,0:T(8,128)(2,1)S(1)}, u32[]{:S(2)}, u32[]{:S(2)}) async-start(bf16[16,256,160]{1,2,0:T(8,128)(2,1)} %broadcast_in_dim.26), calls=%async_computation.2 | async-start | bytes 2621440 | tf_op jit(solution)/shard_map/all_to_all | solution.py:13
  107.9 7.9 %copy-start.9 = (bf16[128,256]{1,0:T(8,128)(2,1)S(1)}, bf16[128,256]{1,0:T(8,128)(2,1)}, u32[]{:S(2)}) copy-start(bf16[128,256]{1,0:T(8,128)(2,1)} %param.25) | copy-start | bytes 196612
  110.2 23.0 %all-to-all-start.1 = ((bf16[16,128,256]{2,1,0:T(8,128)(2,1)}), bf16[16,128,256]{2,1,0:T(8,128)(2,1)S(1)}, u32[]{:S(2)}, u32[]{:S(2)}) async-start(bf16[16,128,256]{2,1,0:T(8,128)(2,1)} %bitcast.691), calls=%async_computation.1 | async-start | bytes 2097152 | tf_op jit(solution)/shard_map/all_to_all | solution.py:108
  115.7 23.2 %copy-start.14 = (s32[8]{0:T(128)S(1)}, s32[8]{0:T(128)}, u32[]{:S(2)}) copy-start(s32[8]{0:T(128)} %param.18) | copy-start | bytes 100
  134.4 20.1 %all-to-all-start.3 = ((bf16[16,128,256]{1,2,0:T(8,128)(2,1)}), bf16[16,128,256]{1,2,0:T(8,128)(2,1)}, u32[]{:S(2)}, u32[]{:S(2)}) async-start(bf16[16,128,256]{1,2,0:T(8,128)(2,1)} %broadcast_in_dim.27), calls=%async_computation.3 | async-start | bytes 2097152 | tf_op jit(solution)/shard_map/all_to_all | solution.py:13
  222.9 27.5 %copy-start.10 = (f32[4096]{0:T(1024)S(1)}, f32[4096]{0:T(1024)}, u32[]{:S(2)}) copy-start(f32[4096]{0:T(1024)} %param.28) | copy-start | bytes 49156
  224.0 13.7 %all-to-all-start.5 = ((f32[2,16,16,256]{3,1,0,2:T(8,128)}), f32[2,16,16,256]{3,1,0,2:T(8,128)S(1)}, u32[]{:S(2)}, u32[]{:S(2)}) async-start(f32[2,16,16,256]{3,1,0,2:T(8,128)} %copy.165), calls=%async_computation.5 | async-start | bytes 1048576 | tf_op jit(solution)/shard_map/all_to_all | solution.py:133
  246.8 12.2 %all-to-all-start.6 = ((f32[16,16,256]{2,0,1:T(8,128)}), f32[16,16,256]{2,0,1:T(8,128)S(1)}, u32[]{:S(2)}, u32[]{:S(2)}) async-start(f32[16,16,256]{2,0,1:T(8,128)} %constant_dynamic-update-slice_fusion), calls=%async_computation.6 | async-start | bytes 524288 | tf_op jit(solution)/shard_map/all_to_all | solution.py:140
  304.7 4.0 copy-start.7
  304.7 16.9 %all-to-all-start.7 = ((bf16[128,16,256]{2,0,1:T(8,128)(2,1)}), bf16[128,16,256]{2,0,1:T(8,128)(2,1)S(1)}, u32[]{:S(2)}, u32[]{:S(2)}) async-start(bf16[128,16,256]{2,0,1:T(8,128)(2,1)} %fusion.33), calls=%async_computation.7 | async-start | bytes 2097152 | tf_op jit(solution)/shard_map/all_to_all | solution.py:145
  322.7 20.2 %all-to-all-start.8 = ((bf16[8,256,256]{1,2,0:T(8,128)(2,1)}), bf16[8,256,256]{1,2,0:T(8,128)(2,1)S(1)}, u32[]{:S(2)}, u32[]{:S(2)}) async-start(bf16[8,256,256]{1,2,0:T(8,128)(2,1)} %broadcast_in_dim.29), calls=%async_computation.8 | async-start | bytes 2097152 | tf_op jit(solution)/shard_map/all_to_all | solution.py:13
  327.0 103.6 %reduce-scatter.2.cloned.1.call-start = ((), (), s32[]{:S(2)}) async-start(), calls=%async_computation.12 | async-start | bytes 8912896 | tf_op jit(solution)/shard_map/reduce_scatter | solution.py:149
  348.6 4.1 copy-start.15
  348.6 82.1 %copy-start = (bf16[1,128,2048]{2,1,0:T(8,128)(2,1)S(1)}, bf16[1,128,2048]{2,1,0:T(8,128)(2,1)}, u32[]{:S(2)}) copy-start(bf16[1,128,2048]{2,1,0:T(8,128)(2,1)} %param.17) | copy-start | bytes 1572868
  349.2 9.4 %all-to-all-start.9 = ((f32[8,1,16,256]{3,2,1,0:T(8,128)}), f32[8,1,16,256]{3,2,1,0:T(8,128)S(1)}, u32[]{:S(2)}, u32[]{:S(2)}) async-start(f32[8,1,16,256]{3,2,1,0:T(8,128)} %broadcast_in_dim.31), calls=%async_computation.10 | async-start | bytes 262144 | tf_op jit(solution)/shard_map/all_to_all | solution.py:13
  (4 other events, 7.5 us)
Sparse Core Ops, SparseCore 0:
  11.4 87.3 all-gather.1
  348.7 81.8 reduce-scatter.1
where the time goes:
time: 441 us; the launch traced here: 439 us
  waiting for transfers between devices  218 us (49%)
  local copies, waits for them, and re-layouts  83.7 us (19%)
  other arithmetic  59.4 us (13%)
  starting transfers between devices  45.1 us (10%)
  matrix products  17.2 us (4%)
  between operations  14.4 us (3%)
    reduce_scatter x1, waiting for transfers between devices, per_device(): lax.psum_scatter(jnp.dot(gated_ch, w_out, preferred_element_type=jnp.floa...  71.3 us
    all_to_all x6, waiting for transfers between devices, gather_a2a(): lax.all_to_all(copies, axis, split_axis=0, concat_axis=0, tiled=True)  64.8 us
    all_gather x1, waiting for transfers between devices, per_device(): lax.all_gather(normed, 'seq', axis=0, tiled=True)  33.5 us
    all_to_all x6, starting transfers between devices, gather_a2a(): lax.all_to_all(copies, axis, split_axis=0, concat_axis=0, tiled=True)  28.4 us
    dynamic_update_slice x32, local copies, waits for them, and re-layouts, piece_scan(): lax.scan(advance, start, (to_blocks(rates), to_blocks(values), to_blocks(...  21.3 us
    reduce_sum x48, other arithmetic, advance(): outputs.append(jnp.sum(outof[:, place][:, :, None] * state, axis=1))  19.8 us
    all_to_all x1, waiting for transfers between devices, per_device(): lax.all_to_all(inner, 'seq', split_axis=0, concat_axis=1, tiled=True)  17.4 us
    squeeze x32, local copies, waits for them, and re-layouts, piece_scan(): lax.scan(advance, start, (to_blocks(rates), to_blocks(values), to_blocks(...  15.9 us
  transfers between devices with their start and end apart: 12, of which 11 were waited for; matrix products, arithmetic and copies ran while one was open for 5% of the time, Pallas kernels for 0%

commit v1 on v0

--- a/solution.py
+++ b/solution.py
@@ -5,6 +5,22 @@
 
 STATE = 16
 RANK = 128
+
+
+def ring_gather(x, axis, dim):
+    ways, here, step = (lax.axis_size(axis), lax.axis_index(axis), x.shape[dim])
+    shape = [n * ways if d == dim else n for d, n in enumerate(x.shape)]
+    full = lax.dynamic_update_slice_in_dim(jnp.zeros(shape, x.dtype), x, here * step, axis=dim)
+    going_up = going_down = x
+    for far in range(1, ways // 2 + 1):
+        going_up = lax.ppermute(going_up, axis, [(d, (d + 1) % ways) for d in range(ways)])
+        full = lax.dynamic_update_slice_in_dim(full, going_up, (here - far) % ways * step, axis=dim)
+        if 2 * far < ways:
+            going_down = lax.ppermute(going_down, axis, [(d, (d - 1) % ways) for d in range(ways)])
+            full = lax.dynamic_update_slice_in_dim(
+                full, going_down, (here + far) % ways * step, axis=dim
+            )
+    return full
 
 
 def gather_a2a(block, axis, dim):
@@ -92,11 +108,7 @@
     normed = (tokens * scale * norm_gain.astype(jnp.float32)).astype(jnp.bfloat16)
     w_in = gather_a2a(in_weight, "req", 1)
     w_flat = jnp.concatenate((w_in[0], w_in[1]), axis=1)
-    both = jnp.dot(
-        lax.all_gather(normed, "seq", axis=0, tiled=True),
-        w_flat,
-        preferred_element_type=jnp.float32,
-    )
+    both = jnp.dot(ring_gather(normed, "seq", 0), w_flat, preferred_element_type=jnp.float32)
     xin = both[:, :width]
     zgate = both[:, width:].astype(jnp.bfloat16)
     padded = jnp.pad(xin, ((taps_count - 1, 0), (0, 0)))

time: 441 us -> 492 us (1.12)
  starting transfers between devices: 45.1 us -> 81.6 us
  local copies, waits for them, and re-layouts: 83.7 us -> 110 us
  waiting for transfers between devices: 218 us -> 205 us
    ppermute x0 -> x15, waiting for transfers between devices: none -> 53.1 us  [the longest x8 32.2 us: ring_gather(): lax.ppermute(going_up, axis, [(d, (d + 1) % ways) for d in range(ways)])]
    ppermute x0 -> x15, starting transfers between devices: none -> 39.8 us  [the longest x7 38.1 us: ring_gather(): lax.ppermute(going_down, axis, [(d, (d - 1) % ways) for d in range(ways)])]
    all_gather x1 -> x0, waiting for transfers between devices: 33.5 us -> none  [per_device(): lax.all_gather(normed, 'seq', axis=0, tiled=True)]
    all_to_all x6, waiting for transfers between devices: 64.8 us -> 36.7 us  [gather_a2a(): lax.all_to_all(copies, axis, split_axis=0, concat_axis=0, tiled=True)]
    dynamic_update_slice x0 -> x15, local copies, waits for them, and re-layouts: none -> 21.2 us  [the longest x8 12.1 us: ring_gather(): lax.dynamic_update_slice_in_dim(full, going_up, (here - far) % ways * ste...]
  transfers between devices with their start and end apart: 12 -> 26, of which waited for: 11 -> 18; matrix products, arithmetic and copies ran while one was open for 5% -> 9% of each run, Pallas kernels for 0% -> 0%
where the time goes in v1:
time: 492 us; the launch traced here: 490 us
  waiting for transfers between devices  205 us (42%)
  local copies, waits for them, and re-layouts  110 us (22%)
  starting transfers between devices  81.6 us (17%)
  other arithmetic  58.4 us (12%)
  matrix products  18.5 us (4%)
  between operations  14.5 us (3%)
    reduce_scatter x1, waiting for transfers between devices, per_device(): lax.psum_scatter(jnp.dot(gated_ch, w_out, preferred_element_type=jnp.floa...  71 us
    ppermute x7, starting transfers between devices, ring_gather(): lax.ppermute(going_down, axis, [(d, (d - 1) % ways) for d in range(ways)])  38.1 us
    all_to_all x6, waiting for transfers between devices, gather_a2a(): lax.all_to_all(copies, axis, split_axis=0, concat_axis=0, tiled=True)  36.7 us
    ppermute x8, waiting for transfers between devices, ring_gather(): lax.ppermute(going_up, axis, [(d, (d + 1) % ways) for d in range(ways)])  32.2 us
    all_to_all x6, starting transfers between devices, gather_a2a(): lax.all_to_all(copies, axis, split_axis=0, concat_axis=0, tiled=True)  27 us
    dynamic_update_slice x32, local copies, waits for them, and re-layouts, piece_scan(): lax.scan(advance, start, (to_blocks(rates), to_blocks(values), to_blocks(...  21.5 us
    ppermute x7, waiting for transfers between devices, ring_gather(): lax.ppermute(going_down, axis, [(d, (d - 1) % ways) for d in range(ways)])  20.9 us
    reduce_sum x48, other arithmetic, advance(): outputs.append(jnp.sum(outof[:, place][:, :, None] * state, axis=1))  19.8 us
  transfers between devices with their start and end apart: 26, of which 18 were waited for; matrix products, arithmetic and copies ran while one was open for 9% of the time, Pallas kernels for 0%

profile of v1, /device:TPU:0, one launch (start us, length us, event | category | flops | bytes accessed | tf_op | source)
XLA Modules:
  0.0 489.9 jit_solution(9225230851471426846)
XLA Ops:
  16.2 4.9 %collective-permute-start.1 = (bf16[128,2048]{1,0:T(8,128)(2,1)S(1)}, bf16[128,2048]{1,0:T(8,128)(2,1)}, u32[]{:S(2)}, u32[]{:S(2)}) collective-permute-start(bf16[128,2048]{1,0:T(8,128)(2,1)S(1)} %get-tuple-element.230), channel_id=1, source_target_pairs={{0,15},{1,0},{2,1},{3,2},{4,3},{5,4},{6,5},{7,6},{8,7},{9,8},{10,9... | collective-permute-start | bytes 1572872 | tf_op jit(solution)/shard_map/ppermute | solution.py:19
  21.1 11.9 %collective-permute-done = bf16[128,2048]{1,0:T(8,128)(2,1)S(1)} collective-permute-done((bf16[128,2048]{1,0:T(8,128)(2,1)S(1)}, bf16[128,2048]{1,0:T(8,128)(2,1)S(1)}, u32[]{:S(2)}, u32[]{:S(2)}) %collective-permute-start) | collective-permute-done | bytes 524320 | tf_op jit(solution)/shard_map/ppermute | solution.py:16
  38.4 11.2 %collective-permute-done.2 = bf16[128,2048]{1,0:T(8,128)(2,1)} collective-permute-done((bf16[128,2048]{1,0:T(8,128)(2,1)S(1)}, bf16[128,2048]{1,0:T(8,128)(2,1)}, u32[]{:S(2)}, u32[]{:S(2)}) %collective-permute-start.2) | collective-permute-done | bytes 524320 | tf_op jit(solution)/shard_map/ppermute | solution.py:16
  57.4 5.4 %collective-permute-start.5 = (bf16[128,2048]{1,0:T(8,128)(2,1)S(1)}, bf16[128,2048]{1,0:T(8,128)(2,1)S(1)}, u32[]{:S(2)}, u32[]{:S(2)}) collective-permute-start(bf16[128,2048]{1,0:T(8,128)(2,1)S(1)} %collective-permute-done.3), channel_id=1, source_target_pairs={{0,15},{1,0},{2,1},{3,2},{4,3},{5,4},{6,5},{7,6},{8,7},{9,8},{10,9... | collective-permute-start | bytes 1572872 | tf_op jit(solution)/shard_map/ppermute | solution.py:19
  74.7 5.8 %collective-permute-start.7 = (bf16[128,2048]{1,0:T(8,128)(2,1)S(1)}, bf16[128,2048]{1,0:T(8,128)(2,1)}, u32[]{:S(2)}, u32[]{:S(2)}) collective-permute-start(bf16[128,2048]{1,0:T(8,128)(2,1)S(1)} %collective-permute-done.5), channel_id=1, source_target_pairs={{0,15},{1,0},{2,1},{3,2},{4,3},{5,4},{6,5},{7,6},{8,7},{9,8},{10,9... | collective-permute-start | bytes 1572872 | tf_op jit(solution)/shard_map/ppermute | solution.py:19
  84.1 7.4 %collective-permute-done.7 = bf16[128,2048]{1,0:T(8,128)(2,1)} collective-permute-done((bf16[128,2048]{1,0:T(8,128)(2,1)S(1)}, bf16[128,2048]{1,0:T(8,128)(2,1)}, u32[]{:S(2)}, u32[]{:S(2)}) %collective-permute-start.7) | collective-permute-done | bytes 524320 | tf_op jit(solution)/shard_map/ppermute | solution.py:19
  91.5 5.9 %collective-permute-start.9 = (bf16[128,2048]{1,0:T(8,128)(2,1)}, bf16[128,2048]{1,0:T(8,128)(2,1)}, u32[]{:S(2)}, u32[]{:S(2)}) collective-permute-start(bf16[128,2048]{1,0:T(8,128)(2,1)} %collective-permute-done.7), channel_id=1, source_target_pairs={{0,15},{1,0},{2,1},{3,2},{4,3},{5,4},{6,5},{7,6},{8,7},{9,8},{10,9... | collective-permute-start | bytes 1572872 | tf_op jit(solution)/shard_map/ppermute | solution.py:19
  97.4 6.7 %all-to-all-start.4 = ((bf16[16,2,128]{2,1,0:T(2,128)(2,1)}), bf16[16,2,128]{2,1,0:T(2,128)(2,1)S(1)}, u32[]{:S(2)}, u32[]{:S(2)}) async-start(bf16[16,2,128]{2,1,0:T(2,128)(2,1)} %reshape.2341), calls=%async_computation.4 | async-start | bytes 16384 | tf_op jit(solution)/shard_map/all_to_all | solution.py:29
  107.9 5.8 %collective-permute-start.11 = (bf16[128,2048]{1,0:T(8,128)(2,1)}, bf16[128,2048]{1,0:T(8,128)(2,1)S(1)}, u32[]{:S(2)}, u32[]{:S(2)}) collective-permute-start(bf16[128,2048]{1,0:T(8,128)(2,1)} %collective-permute-done.9), channel_id=1, source_target_pairs={{0,15},{1,0},{2,1},{3,2},{4,3},{5,4},{6,5},{7,6},{8,7},{9,8},{10,9... | collective-permute-start | bytes 1572872 | tf_op jit(solution)/shard_map/ppermute | solution.py:19
  123.2 5.7 %collective-permute-start.13 = (bf16[128,2048]{1,0:T(8,128)(2,1)S(1)}, bf16[128,2048]{1,0:T(8,128)(2,1)S(1)}, u32[]{:S(2)}, u32[]{:S(2)}) collective-permute-start(bf16[128,2048]{1,0:T(8,128)(2,1)S(1)} %collective-permute-done.11), channel_id=1, source_target_pairs={{0,15},{1,0},{2,1},{3,2},{4,3},{5,4},{6,5},{7,6},{8,7},{9,8},{10,9... | collective-permute-start | bytes 1572872 | tf_op jit(solution)/shard_map/ppermute | solution.py:19
  138.1 6.6 %collective-permute-done.14 = bf16[128,2048]{1,0:T(8,128)(2,1)S(1)} collective-permute-done((bf16[128,2048]{1,0:T(8,128)(2,1)S(1)}, bf16[128,2048]{1,0:T(8,128)(2,1)S(1)}, u32[]{:S(2)}, u32[]{:S(2)}) %collective-permute-start.14) | collective-permute-done | bytes 524320 | tf_op jit(solution)/shard_map/ppermute | solution.py:16
  150.6 7.2 %fusion.29 = f32[2048,512]{1,0:T(8,128)S(1)} fusion(bf16[2048,2048]{1,0:T(8,128)(2,1)} %constant_dynamic-update-slice_fusion.16, bf16[2048,256]{1,0:T(8,128)(2,1)} %bitcast.737, bf16[2048,256]{1,0:T(8,128)(2,1)S(1)} %bitcast.736), kind=kOutput, calls=%fused_computation.84 | convolution fusion | flops 4299161600 | bytes 14680064 | tf_op jit(solution)/shard_map/dot_general | solution.py:111
  162.1 5.6 %all-to-all-done.2 = bf16[16,256,160]{1,2,0:T(8,128)(2,1)S(1)} async-done(((bf16[16,256,160]{1,2,0:T(8,128)(2,1)}), bf16[16,256,160]{1,2,0:T(8,128)(2,1)S(1)}, u32[]{:S(2)}, u32[]{:S(2)}) %all-to-all-start.2) | async-done | bytes 1310752 | tf_op jit(solution)/shard_map/all_to_all | solution.py:29
  171.5 13.2 %all-to-all-done.1 = bf16[16,128,256]{2,1,0:T(8,128)(2,1)S(1)} async-done(((bf16[16,128,256]{2,1,0:T(8,128)(2,1)}), bf16[16,128,256]{2,1,0:T(8,128)(2,1)S(1)}, u32[]{:S(2)}, u32[]{:S(2)}) %all-to-all-start.1) | async-done | bytes 1048608 | tf_op jit(solution)/shard_map/all_to_all | solution.py:120
  192.0 11.5 %all-to-all-done.3 = bf16[16,128,256]{1,2,0:T(8,128)(2,1)} async-done(((bf16[16,128,256]{1,2,0:T(8,128)(2,1)}), bf16[16,128,256]{1,2,0:T(8,128)(2,1)}, u32[]{:S(2)}, u32[]{:S(2)}) %all-to-all-start.3) | async-done | bytes 1048608 | tf_op jit(solution)/shard_map/all_to_all | solution.py:29
  216.6 55.3 %while.24 = (s32[]{:T(128)}, f32[1,16,4096]{2,1,0:T(8,128)S(1)}, f32[16,1,8,4096]{3,2,1,0:T(8,128)}, f32[16,1,8,4096]{3,2,1,0:T(8,128)}, f32[16,4096]{1,0:T(8,12...) while((s32[]{:T(128)}, f32[1,16,4096]{2,1,0:T(8,128)S(1)}, ...), condition=%wide.region_10.11_spmd.clone, body=%wide.region_1.10_spmd.clone.sunk | while | flops 4849667 | bytes 4347896 | solution.py:66
  277.7 9.3 %all-to-all-done.5 = f32[2,16,16,256]{3,1,0,2:T(8,128)S(1)} async-done(((f32[2,16,16,256]{3,1,0,2:T(8,128)}), f32[2,16,16,256]{3,1,0,2:T(8,128)S(1)}, u32[]{:S(2)}, u32[]{:S(2)}) %all-to-all-start.5) | async-done | bytes 524320 | tf_op jit(solution)/shard_map/all_to_all | solution.py:145
  299.6 8.6 %all-to-all-done.6 = f32[16,16,256]{2,0,1:T(8,128)S(1)} async-done(((f32[16,16,256]{2,0,1:T(8,128)}), f32[16,16,256]{2,0,1:T(8,128)S(1)}, u32[]{:S(2)}, u32[]{:S(2)}) %all-to-all-start.6) | async-done | bytes 262176 | tf_op jit(solution)/shard_map/all_to_all | solution.py:152
  310.0 38.5 %while.23 = (s32[]{:T(128)}, f32[16,1,8,4096]{3,2,1,0:T(8,128)}, f32[16,1,8,16]{3,2,1,0:T(8,128)S(1)}, f32[16,1,8,4096]{3,2,1,0:T(8,128)}, f32[16,4096]{1,0:T(8,128)S(1)}, /*index=5*/f32[16,16,256]{2,1,0:T(8,128)S(1)}, s32[]{:T(128)}) while((s32[]{:T(128)}, f32[16,1,8,4096]{3,2,1,0:T(8,128)}, f32[16,1,8,16]{3,2,1,0:T(8,128)S(1)}, ...), condition=%wide.region_13.14_spmd, body=%wide.region_11.13_spmd.sunk | while | flops 2064386 | bytes 1837141 | solution.py:80
  358.0 13.2 %all-to-all-done.7 = bf16[128,16,256]{2,0,1:T(8,128)(2,1)S(1)} async-done(((bf16[128,16,256]{2,0,1:T(8,128)(2,1)}), bf16[128,16,256]{2,0,1:T(8,128)(2,1)S(1)}, u32[]{:S(2)}, u32[]{:S(2)}) %all-to-all-start.7) | async-done | bytes 1048608 | tf_op jit(solution)/shard_map/all_to_all | solution.py:157
  378.8 13.6 %all-to-all-done.8 = bf16[8,256,256]{1,2,0:T(8,128)(2,1)} async-done(((bf16[8,256,256]{1,2,0:T(8,128)(2,1)}), bf16[8,256,256]{1,2,0:T(8,128)(2,1)}, u32[]{:S(2)}, u32[]{:S(2)}) %all-to-all-start.8) | async-done | bytes 1048608 | tf_op jit(solution)/shard_map/all_to_all | solution.py:29
  392.4 6.9 %convolution_convert_fusion = bf16[2048,2048]{1,0:T(8,128)(2,1)} fusion(bf16[2048,256]{1,0:T(8,128)(2,1)S(1)} %fusion.36, bf16[256,2048]{0,1:T(8,128)(2,1)} %bitcast.65), kind=kOutput, calls=%fused_computation.73 | convolution fusion | flops 2151677952 | bytes 10485760 | tf_op jit(solution)/shard_map/dot_general | solution.py:162
  403.4 6.0 %all-to-all-done.9 = f32[8,1,16,256]{3,2,1,0:T(8,128)S(1)} async-done(((f32[8,1,16,256]{3,2,1,0:T(8,128)}), f32[8,1,16,256]{3,2,1,0:T(8,128)S(1)}, u32[]{:S(2)}, u32[]{:S(2)}) %all-to-all-start.9) | async-done | bytes 131104 | tf_op jit(solution)/shard_map/all_to_all | solution.py:29
  410.1 71.0 %reduce-scatter.2.cloned.1.call-done = bf16[128,2048]{1,0:T(8,128)(2,1)} async-done(((bf16[2048,2048]{1,0:T(8,128)(2,1)}), bf16[128,2048]{1,0:T(8,128)(2,1)}) %reduce-scatter.2.cloned.1.call-update) | async-done | bytes 524304 | tf_op jit(solution)/shard_map/reduce_scatter | solution.py:161
  (411 shorter events, 230.6 us)
Async XLA Ops:
  14.4 18.6 %collective-permute-start = (bf16[128,2048]{1,0:T(8,128)(2,1)S(1)}, bf16[128,2048]{1,0:T(8,128)(2,1)S(1)}, u32[]{:S(2)}, u32[]{:S(2)}) collective-permute-start(bf16[128,2048]{1,0:T(8,128)(2,1)S(1)} %get-tuple-element.230), channel_id=1, source_target_pairs={{0,1},{1,2},{2,3},{3,4},{4,5},{5,6},{6,7},{7,8},{8,9},{9,10},{10,1... | collective-permute-start | bytes 1572872 | tf_op jit(solution)/shard_map/ppermute | solution.py:16
  16.2 17.6 %collective-permute-start.1 = (bf16[128,2048]{1,0:T(8,128)(2,1)S(1)}, bf16[128,2048]{1,0:T(8,128)(2,1)}, u32[]{:S(2)}, u32[]{:S(2)}) collective-permute-start(bf16[128,2048]{1,0:T(8,128)(2,1)S(1)} %get-tuple-element.230), channel_id=1, source_target_pairs={{0,15},{1,0},{2,1},{3,2},{4,3},{5,4},{6,5},{7,6},{8,7},{9,8},{10,9... | collective-permute-start | bytes 1572872 | tf_op jit(solution)/shard_map/ppermute | solution.py:19
  33.0 16.5 %collective-permute-start.2 = (bf16[128,2048]{1,0:T(8,128)(2,1)S(1)}, bf16[128,2048]{1,0:T(8,128)(2,1)}, u32[]{:S(2)}, u32[]{:S(2)}) collective-permute-start(bf16[128,2048]{1,0:T(8,128)(2,1)S(1)} %collective-permute-done), channel_id=1, source_target_pairs={{0,1},{1,2},{2,3},{3,4},{4,5},{5,6},{6,7},{7,8},{8,9},{9,10},{10,1... | collective-permute-start | bytes 1572872 | tf_op jit(solution)/shard_map/ppermute | solution.py:16
  33.8 23.6 %collective-permute-start.3 = (bf16[128,2048]{1,0:T(8,128)(2,1)}, bf16[128,2048]{1,0:T(8,128)(2,1)S(1)}, u32[]{:S(2)}, u32[]{:S(2)}) collective-permute-start(bf16[128,2048]{1,0:T(8,128)(2,1)} %collective-permute-done.1), channel_id=1, source_target_pairs={{0,15},{1,0},{2,1},{3,2},{4,3},{5,4},{6,5},{7,6},{8,7},{9,8},{10,9... | collective-permute-start | bytes 1572872 | tf_op jit(solution)/shard_map/ppermute | solution.py:19
  49.5 15.9 %collective-permute-start.4 = (bf16[128,2048]{1,0:T(8,128)(2,1)}, bf16[128,2048]{1,0:T(8,128)(2,1)}, u32[]{:S(2)}, u32[]{:S(2)}) collective-permute-start(bf16[128,2048]{1,0:T(8,128)(2,1)} %collective-permute-done.2), channel_id=1, source_target_pairs={{0,1},{1,2},{2,3},{3,4},{4,5},{5,6},{6,7},{7,8},{8,9},{9,10},{10,1... | collective-permute-start | bytes 1572872 | tf_op jit(solution)/shard_map/ppermute | solution.py:16
  51.1 46.3 %all-to-all-start = ((bf16[8,2,256,256]{3,2,1,0:T(8,128)(2,1)}), bf16[8,2,256,256]{3,2,1,0:T(8,128)(2,1)S(1)}, u32[]{:S(2)}, u32[]{:S(2)}) async-start(bf16[8,2,256,256]{3,2,1,0:T(8,128)(2,1)} %broadcast_in_dim.28), calls=%async_computation | async-start | bytes 4194304 | tf_op jit(solution)/shard_map/all_to_all | solution.py:29
  57.4 17.3 %collective-permute-start.5 = (bf16[128,2048]{1,0:T(8,128)(2,1)S(1)}, bf16[128,2048]{1,0:T(8,128)(2,1)S(1)}, u32[]{:S(2)}, u32[]{:S(2)}) collective-permute-start(bf16[128,2048]{1,0:T(8,128)(2,1)S(1)} %collective-permute-done.3), channel_id=1, source_target_pairs={{0,15},{1,0},{2,1},{3,2},{4,3},{5,4},{6,5},{7,6},{8,7},{9,8},{10,9... | collective-permute-start | bytes 1572872 | tf_op jit(solution)/shard_map/ppermute | solution.py:19
  65.4 15.1 %collective-permute-start.6 = (bf16[128,2048]{1,0:T(8,128)(2,1)}, bf16[128,2048]{1,0:T(8,128)(2,1)S(1)}, u32[]{:S(2)}, u32[]{:S(2)}) collective-permute-start(bf16[128,2048]{1,0:T(8,128)(2,1)} %collective-permute-done.4), channel_id=1, source_target_pairs={{0,1},{1,2},{2,3},{3,4},{4,5},{5,6},{6,7},{7,8},{8,9},{9,10},{10,1... | collective-permute-start | bytes 1572872 | tf_op jit(solution)/shard_map/ppermute | solution.py:16
  74.7 16.8 %collective-permute-start.7 = (bf16[128,2048]{1,0:T(8,128)(2,1)S(1)}, bf16[128,2048]{1,0:T(8,128)(2,1)}, u32[]{:S(2)}, u32[]{:S(2)}) collective-permute-start(bf16[128,2048]{1,0:T(8,128)(2,1)S(1)} %collective-permute-done.5), channel_id=1, source_target_pairs={{0,15},{1,0},{2,1},{3,2},{4,3},{5,4},{6,5},{7,6},{8,7},{9,8},{10,9... | collective-permute-start | bytes 1572872 | tf_op jit(solution)/shard_map/ppermute | solution.py:19
  80.5 16.9 %collective-permute-start.8 = (bf16[128,2048]{1,0:T(8,128)(2,1)S(1)}, bf16[128,2048]{1,0:T(8,128)(2,1)}, u32[]{:S(2)}, u32[]{:S(2)}) collective-permute-start(bf16[128,2048]{1,0:T(8,128)(2,1)S(1)} %collective-permute-done.6), channel_id=1, source_target_pairs={{0,1},{1,2},{2,3},{3,4},{4,5},{5,6},{6,7},{7,8},{8,9},{9,10},{10,1... | collective-permute-start | bytes 1572872 | tf_op jit(solution)/shard_map/ppermute | solution.py:16
  91.5 16.5 %collective-permute-start.9 = (bf16[128,2048]{1,0:T(8,128)(2,1)}, bf16[128,2048]{1,0:T(8,128)(2,1)}, u32[]{:S(2)}, u32[]{:S(2)}) collective-permute-start(bf16[128,2048]{1,0:T(8,128)(2,1)} %collective-permute-done.7), channel_id=1, source_target_pairs={{0,15},{1,0},{2,1},{3,2},{4,3},{5,4},{6,5},{7,6},{8,7},{9,8},{10,9... | collective-permute-start | bytes 1572872 | tf_op jit(solution)/shard_map/ppermute | solution.py:19
  97.4 18.2 %collective-permute-start.10 = (bf16[128,2048]{1,0:T(8,128)(2,1)}, bf16[128,2048]{1,0:T(8,128)(2,1)}, u32[]{:S(2)}, u32[]{:S(2)}) collective-permute-start(bf16[128,2048]{1,0:T(8,128)(2,1)} %collective-permute-done.8), channel_id=1, source_target_pairs={{0,1},{1,2},{2,3},{3,4},{4,5},{5,6},{6,7},{7,8},{8,9},{9,10},{10,1... | collective-permute-start | bytes 1572872 | tf_op jit(solution)/shard_map/ppermute | solution.py:16
  97.4 48.1 %all-to-all-start.4 = ((bf16[16,2,128]{2,1,0:T(2,128)(2,1)}), bf16[16,2,128]{2,1,0:T(2,128)(2,1)S(1)}, u32[]{:S(2)}, u32[]{:S(2)}) async-start(bf16[16,2,128]{2,1,0:T(2,128)(2,1)} %reshape.2341), calls=%async_computation.4 | async-start | bytes 16384 | tf_op jit(solution)/shard_map/all_to_all | solution.py:29
  107.9 15.3 %collective-permute-start.11 = (bf16[128,2048]{1,0:T(8,128)(2,1)}, bf16[128,2048]{1,0:T(8,128)(2,1)S(1)}, u32[]{:S(2)}, u32[]{:S(2)}) collective-permute-start(bf16[128,2048]{1,0:T(8,128)(2,1)} %collective-permute-done.9), channel_id=1, source_target_pairs={{0,15},{1,0},{2,1},{3,2},{4,3},{5,4},{6,5},{7,6},{8,7},{9,8},{10,9... | collective-permute-start | bytes 1572872 | tf_op jit(solution)/shard_map/ppermute | solution.py:19
  115.6 15.2 %collective-permute-start.12 = (bf16[128,2048]{1,0:T(8,128)(2,1)}, bf16[128,2048]{1,0:T(8,128)(2,1)S(1)}, u32[]{:S(2)}, u32[]{:S(2)}) collective-permute-start(bf16[128,2048]{1,0:T(8,128)(2,1)} %collective-permute-done.10), channel_id=1, source_target_pairs={{0,1},{1,2},{2,3},{3,4},{4,5},{5,6},{6,7},{7,8},{8,9},{9,10},{10,1... | collective-permute-start | bytes 1572872 | tf_op jit(solution)/shard_map/ppermute | solution.py:16
  123.2 14.1 %collective-permute-start.13 = (bf16[128,2048]{1,0:T(8,128)(2,1)S(1)}, bf16[128,2048]{1,0:T(8,128)(2,1)S(1)}, u32[]{:S(2)}, u32[]{:S(2)}) collective-permute-start(bf16[128,2048]{1,0:T(8,128)(2,1)S(1)} %collective-permute-done.11), channel_id=1, source_target_pairs={{0,15},{1,0},{2,1},{3,2},{4,3},{5,4},{6,5},{7,6},{8,7},{9,8},{10,9... | collective-permute-start | bytes 1572872 | tf_op jit(solution)/shard_map/ppermute | solution.py:19
  130.8 13.9 %collective-permute-start.14 = (bf16[128,2048]{1,0:T(8,128)(2,1)S(1)}, bf16[128,2048]{1,0:T(8,128)(2,1)S(1)}, u32[]{:S(2)}, u32[]{:S(2)}) collective-permute-start(bf16[128,2048]{1,0:T(8,128)(2,1)S(1)} %collective-permute-done.12), channel_id=1, source_target_pairs={{0,1},{1,2},{2,3},{3,4},{4,5},{5,6},{6,7},{7,8},{8,9},{9,10},{10,1... | collective-permute-start | bytes 1572872 | tf_op jit(solution)/shard_map/ppermute | solution.py:16
  146.7 21.0 %all-to-all-start.2 = ((bf16[16,256,160]{1,2,0:T(8,128)(2,1)}), bf16[16,256,160]{1,2,0:T(8,128)(2,1)S(1)}, u32[]{:S(2)}, u32[]{:S(2)}) async-start(bf16[16,256,160]{1,2,0:T(8,128)(2,1)} %broadcast_in_dim.29), calls=%async_computation.2 | async-start | bytes 2621440 | tf_op jit(solution)/shard_map/all_to_all | solution.py:29
  167.7 17.0 %all-to-all-start.1 = ((bf16[16,128,256]{2,1,0:T(8,128)(2,1)}), bf16[16,128,256]{2,1,0:T(8,128)(2,1)S(1)}, u32[]{:S(2)}, u32[]{:S(2)}) async-start(bf16[16,128,256]{2,1,0:T(8,128)(2,1)} %bitcast.692), calls=%async_computation.1 | async-start | bytes 2097152 | tf_op jit(solution)/shard_map/all_to_all | solution.py:120
  185.9 17.7 %all-to-all-start.3 = ((bf16[16,128,256]{1,2,0:T(8,128)(2,1)}), bf16[16,128,256]{1,2,0:T(8,128)(2,1)}, u32[]{:S(2)}, u32[]{:S(2)}) async-start(bf16[16,128,256]{1,2,0:T(8,128)(2,1)} %broadcast_in_dim.30), calls=%async_computation.3 | async-start | bytes 2097152 | tf_op jit(solution)/shard_map/all_to_all | solution.py:29
  273.3 13.7 %all-to-all-start.5 = ((f32[2,16,16,256]{3,1,0,2:T(8,128)}), f32[2,16,16,256]{3,1,0,2:T(8,128)S(1)}, u32[]{:S(2)}, u32[]{:S(2)}) async-start(f32[2,16,16,256]{3,1,0,2:T(8,128)} %copy.165), calls=%async_computation.5 | async-start | bytes 1048576 | tf_op jit(solution)/shard_map/all_to_all | solution.py:145
  354.0 17.1 %all-to-all-start.7 = ((bf16[128,16,256]{2,0,1:T(8,128)(2,1)}), bf16[128,16,256]{2,0,1:T(8,128)(2,1)S(1)}, u32[]{:S(2)}, u32[]{:S(2)}) async-start(bf16[128,16,256]{2,0,1:T(8,128)(2,1)} %fusion.33), calls=%async_computation.7 | async-start | bytes 2097152 | tf_op jit(solution)/shard_map/all_to_all | solution.py:157
  372.2 20.2 %all-to-all-start.8 = ((bf16[8,256,256]{1,2,0:T(8,128)(2,1)}), bf16[8,256,256]{1,2,0:T(8,128)(2,1)}, u32[]{:S(2)}, u32[]{:S(2)}) async-start(bf16[8,256,256]{1,2,0:T(8,128)(2,1)} %broadcast_in_dim.32), calls=%async_computation.8 | async-start | bytes 2097152 | tf_op jit(solution)/shard_map/all_to_all | solution.py:29
  376.5 104.6 %reduce-scatter.2.cloned.1.call-start = ((), (), s32[]{:S(2)}) async-start(), calls=%async_computation.11 | async-start | bytes 8912896 | tf_op jit(solution)/shard_map/reduce_scatter | solution.py:161
  (21 other events, 194.2 us)
Sparse Core Ops, SparseCore 0:
  399.5 81.5 reduce-scatter.1
